TPU v7x, 512 devices: a whole 4x4x16 slice. The times are simulated.
512 devices in a mesh: req: 16 (over z), tp: 32 (over x, y, core).
Axes of the slice: x: 4, y: 4, z: 16, core: 2. Of those that a mesh axis runs over, the one named last changes fastest.
Arguments:
- hidden: bfloat16 [1024, 5120], P(('req', 'tp')), may hold values from -6 to 6
- input_norm_gain: float32 [5120], replicated, may hold values from 0.1 to 1.9
- query_weight: bfloat16 [5120, 4096], P(None, 'tp'), may hold values from -1 to 1
- key_weight: bfloat16 [128, 8, 5120], P('tp'), may hold values from -0.078125 to 0.078125
- value_weight: bfloat16 [128, 8, 5120], P('tp'), may hold values from -0.078125 to 0.078125
- output_weight: bfloat16 [4096, 5120], P('tp'), may hold values from -0.09375 to 0.09375
- query_bias_vector: float32 [4096], P('tp'), may hold values from -3 to 3
- value_bias_vector: float32 [128, 8], P('tp'), may hold values from -3 to 3
- adapter_down_maps: bfloat16 [16, 5120, 32], P('req', 'tp'), may hold values from -0.078125 to 0.078125
- adapter_query_up: bfloat16 [16, 16, 4096], P('req', None, 'tp'), may hold values from -1.5 to 1.5
- adapter_value_up: bfloat16 [16, 16, 128, 8], P('req', None, 'tp'), may hold values from -1.5 to 1.5
- lengths: int32 [16, 8], P('req'), may hold values from 1 to 32, 64 in all within a row
- prompt_adapter: int32 [16, 8], P('req'), may hold values from 0 to 15
Outputs:
- output: bfloat16 [1024, 5120], P(('req', 'tp'))
All inputs are finite; a program needn't handle non-finite values.
Results may differ from a plain program's by a relative error of at most 0.019.
Values may be sent and summed in bfloat16 or wider, within the bound.
No kernel may reach another device: no remote copies, remote signals or barrier semaphores. Data moves between devices by JAX's collectives and lax.ppermute only.
A program may use at most 128 MiB of HBM per device.

v0:
```python
import jax
import jax.numpy as jnp
from jax import lax
from jax.sharding import PartitionSpec as P

HD = 128
HK = 8
HQ = 32
eps = 1e-06
rope_base = 1000000.0


def prompt_layout(prompt_length_list, group_tokens):
    count = prompt_length_list.shape[0]
    prompts = jnp.arange(count, dtype=jnp.int32)
    ends = jnp.sum(
        jnp.where(prompts[None, :] <= prompts[:, None], prompt_length_list[None, :], 0), axis=1
    )
    starts = ends - prompt_length_list
    places = jnp.arange(group_tokens, dtype=jnp.int32)
    group_entry = (places[:, None] >= starts[None, :]) & (places[:, None] < ends[None, :])
    segment = jnp.sum(jnp.where(group_entry, prompts[None, :], 0), axis=1)
    offset = places - jnp.sum(jnp.where(group_entry, starts[None, :], 0), axis=1)
    return (group_entry, segment, offset)


def rms_rows(source, input_norm_gain):
    values = source.astype(jnp.float32)
    return (
        values
        * lax.rsqrt(jnp.mean(values * values, axis=-1, keepdims=True) + eps)
        * input_norm_gain
    ).astype(jnp.bfloat16)


def rotate(values, offset):
    width = values.shape[-1]
    half_width = width // 2
    frequency = rope_base ** (-(jnp.arange(half_width, dtype=jnp.float32) * 2.0) / width)
    angles = offset.astype(jnp.float32)[:, None] * frequency[None, :]
    cosine = jnp.cos(angles)[:, None, :]
    sines = jnp.sin(angles)[:, None, :]
    lower_half = values[..., :half_width]
    upper_half = values[..., half_width:]
    return jnp.concatenate(
        [lower_half * cosine - upper_half * sines, upper_half * cosine + lower_half * sines],
        axis=-1,
    )


def rotate_rows(values_t, offset):
    width = values_t.shape[0]
    half_width = width // 2
    frequency = rope_base ** (-(jnp.arange(half_width, dtype=jnp.float32) * 2.0) / width)
    angles = offset.astype(jnp.float32)[None, :] * frequency[:, None]
    cosine = jnp.cos(angles)
    sines = jnp.sin(angles)
    lower_half = values_t[:half_width]
    upper_half = values_t[half_width:]
    return jnp.concatenate(
        [lower_half * cosine - upper_half * sines, upper_half * cosine + lower_half * sines], axis=0
    )


def attend(query_rot, key_rot_t, value_head_t, segment):
    scores = jnp.einsum(
        "qhd,dk->hqk", query_rot, key_rot_t, preferred_element_type=jnp.float32
    ) * HD ** (-0.5)
    places = jnp.arange(segment.shape[0], dtype=jnp.int32)
    allowed = (segment[:, None] == segment[None, :]) & (places[None, :] <= places[:, None])
    scores = jnp.where(allowed[None], scores, jnp.float32(-1e30))
    row_max = jnp.max(scores, axis=-1, keepdims=True)
    weights = jnp.exp(scores - row_max)
    probabilities = (weights / jnp.sum(weights, axis=-1, keepdims=True)).astype(jnp.bfloat16)
    mixed = jnp.einsum(
        "hqk,dk->qhd", probabilities, value_head_t, preferred_element_type=jnp.float32
    )
    return mixed.astype(jnp.bfloat16)


def shards(
    hidden,
    input_norm_gain,
    query_weight,
    key_weight,
    value_weight,
    output_weight,
    query_bias_vector,
    value_bias_vector,
    adapter_down_maps,
    adapter_query_up,
    adapter_value_up,
    lengths,
    prompt_adapter,
):
    tp_width = lax.axis_size("tp")
    tp_place = lax.axis_index("tp")
    tok_rows = hidden.shape[0]
    group_tokens = tok_rows * tp_width
    rank_extent = adapter_query_up.shape[1]
    entry_slice = key_weight.shape[0]
    kv_heads = key_weight.shape[1]
    feat_slice = adapter_down_maps.shape[1]
    head_count = query_weight.shape[1] // HD
    down_flat = adapter_down_maps.reshape(1, -1)
    query_flat = adapter_query_up.reshape(1, -1)
    value_flat = adapter_value_up.reshape(1, -1)
    bank_piece = jnp.concatenate([down_flat, query_flat, value_flat], axis=1)
    req_width = lax.axis_size("req")
    bank = lax.all_to_all(jnp.tile(bank_piece, (req_width, 1)), "req", 0, 0, tiled=True)
    adapter_total = bank.shape[0]
    n_down, n_query = (down_flat.shape[1], query_flat.shape[1])
    bank_down = bank[:, :n_down].reshape((adapter_total,) + adapter_down_maps.shape[1:])
    bank_query = bank[:, n_down : n_down + n_query].reshape(
        (adapter_total,) + adapter_query_up.shape[1:]
    )
    bank_value = bank[:, n_down + n_query :].reshape((adapter_total,) + adapter_value_up.shape[1:])
    prompt_length_list = lengths[0]
    adapter_choice_list = prompt_adapter[0]
    group_entry, segment, offset = prompt_layout(prompt_length_list, group_tokens)
    token_adapter = jnp.sum(jnp.where(group_entry, adapter_choice_list[None, :], 0), axis=1)
    adapter_pick = token_adapter[:, None] == jnp.arange(adapter_total, dtype=jnp.int32)[None, :]
    gathered = lax.all_gather(hidden, "tp", axis=0, tiled=True)
    normalized_input = rms_rows(gathered, input_norm_gain)
    own_features = lax.dynamic_slice_in_dim(normalized_input, tp_place * feat_slice, feat_slice, 1)
    terms = jnp.dot(
        own_features,
        jnp.transpose(bank_down, (1, 0, 2)).reshape(feat_slice, -1),
        preferred_element_type=jnp.float32,
    ).reshape(group_tokens, adapter_total, 2 * rank_extent)
    latent_part = jnp.sum(jnp.where(adapter_pick[:, :, None], terms, 0.0), axis=1)
    key_cols = jnp.einsum(
        "tm,ehm->het", normalized_input, key_weight, preferred_element_type=jnp.float32
    )
    value_cols = (
        jnp.einsum(
            "tm,ehm->het", normalized_input, value_weight, preferred_element_type=jnp.float32
        )
        + jnp.transpose(value_bias_vector)[:, :, None]
    )
    per_kv = tp_width // kv_heads
    key_send = jnp.repeat(key_cols, per_kv, axis=0).reshape(tp_width, -1)
    value_send = jnp.repeat(value_cols, per_kv, axis=0).reshape(tp_width, -1)
    latent_send = jnp.broadcast_to(latent_part.reshape(1, -1), (tp_width, latent_part.size))
    up_send = jnp.repeat(
        bank_value.transpose(3, 0, 1, 2).reshape(kv_heads, -1).astype(jnp.float32), per_kv, axis=0
    )
    n_key, n_value, n_latent = (key_send.shape[1], value_send.shape[1], latent_send.shape[1])
    kv_send = jnp.concatenate([key_send, value_send, latent_send, up_send], axis=1)
    kv_width = kv_send.shape[1]
    kv_pad = -kv_width % (8 * 128)
    kv_send = jnp.pad(kv_send, ((0, 0), (0, kv_pad))).reshape(tp_width, -1, 128)
    received = lax.all_to_all(kv_send, "tp", 0, 0, tiled=True).reshape(tp_width, -1)[:, :kv_width]
    key_head_t = received[:, :n_key].reshape(HD, group_tokens).astype(jnp.bfloat16)
    value_base_t = received[:, n_key : n_key + n_value].reshape(HD, group_tokens)
    latent = jnp.sum(
        received[:, n_key + n_value : n_key + n_value + n_latent].reshape(
            tp_width, group_tokens, 2 * rank_extent
        ),
        axis=0,
    ).astype(jnp.bfloat16)
    value_up_rows = received[:, n_key + n_value + n_latent :].reshape(
        tp_width, adapter_total * rank_extent, entry_slice
    )
    pick = adapter_pick.astype(jnp.bfloat16)
    query_latent = (latent[:, None, :rank_extent] * pick[:, :, None]).reshape(group_tokens, -1)
    value_latent = (latent[:, None, rank_extent:] * pick[:, :, None]).reshape(group_tokens, -1)
    query_rows = (
        jnp.dot(normalized_input, query_weight, preferred_element_type=jnp.float32)
        + query_bias_vector
        + jnp.dot(
            query_latent,
            bank_query.reshape(-1, bank_query.shape[-1]),
            preferred_element_type=jnp.float32,
        )
    )
    value_head_t = (
        value_base_t
        + jnp.einsum(
            "ta,sae->set",
            value_latent,
            value_up_rows.astype(jnp.bfloat16),
            preferred_element_type=jnp.float32,
        ).reshape(HD, group_tokens)
    ).astype(jnp.bfloat16)
    key_rot_t = rotate_rows(key_head_t.astype(jnp.float32), offset).astype(jnp.bfloat16)
    query_rot = rotate(query_rows.reshape(group_tokens, head_count, HD), offset).astype(
        jnp.bfloat16
    )
    mixed_heads = attend(query_rot, key_rot_t, value_head_t, segment).reshape(
        group_tokens, head_count * HD
    )
    block_terms = jnp.dot(mixed_heads, output_weight, preferred_element_type=jnp.float32).astype(
        jnp.bfloat16
    )
    owner_terms = lax.all_to_all(
        block_terms.reshape(tp_width, tok_rows, block_terms.shape[-1]), "tp", 0, 0, tiled=True
    )
    projected = jnp.sum(owner_terms.astype(jnp.float32), axis=0)
    return (hidden.astype(jnp.float32) + projected).astype(jnp.bfloat16)


def solution(mesh):
    return jax.shard_map(
        shards,
        mesh=mesh,
        in_specs=(
            P(("req", "tp"), None),
            P(),
            P(None, "tp"),
            P("tp", None, None),
            P("tp", None, None),
            P("tp", None),
            P("tp"),
            P("tp", None),
            P("req", "tp", None),
            P("req", None, "tp"),
            P("req", None, "tp", None),
            P("req", None),
            P("req", None),
        ),
        out_specs=P(("req", "tp"), None),
        check_vma=False,
    )
```

profile of v0, /device:TPU:1, one launch (start us, length us, event | category | flops | bytes accessed | tf_op | source)
XLA Modules:
  0.0 92.9 jit_solution(2929217116227379337)
XLA Ops:
  0.0 0.9 %copy.56 = bf16[1,160,32]{2,1,0:T(8,128)(2,1)S(1)} copy(bf16[1,160,32]{1,2,0:T(8,128)(2,1)} %param.21) | data formatting | bytes 20480 | tf_op args[8]
  1.0 0.1 reshape.350
  1.1 0.8 copy.57
  1.8 0.1 reshape.352
  1.9 0.7 copy.79
  2.6 0.1 maximum_reduce_fusion
  2.7 0.3 tile.2
  3.0 0.5 broadcast.220
  3.5 2.1 %reduce.5 = bf16[16,7680]{1,0:T(8,128)(2,1)S(1)} reduce(bf16[16,1,7680]{2,1,0:T(2,128)(2,1)S(1)} %tile.2, bf16[]{:T(256)} %broadcast.220), dimensions={1}, to_apply=%tile.2.reduce_sub_computation | reduce | bytes 491522 | tf_op jit(solution)/shard_map/tile | solution.py:110
  5.6 0.7 reshape.372
  6.3 15.7 %all-to-all-start = ((bf16[16,2,3840]{2,1,0:T(2,128)(2,1)}), bf16[16,2,3840]{2,1,0:T(2,128)(2,1)S(1)}, u32[]{:S(2)}, u32[]{:S(2)}) async-start(bf16[16,2,3840]{2,1,0:T(2,128)(2,1)} %reshape.372), calls=%async_computation | async-start | bytes 491520 | tf_op jit(solution)/shard_map/all_to_all | solution.py:110
  22.1 26.0 %all-gather = bf16[32,2,5120]{2,1,0:T(2,128)(2,1)S(1)} all-gather(bf16[1,2,5120]{2,1,0:T(2,128)(2,1)S(1)} %bitcast.107), channel_id=1, replica_groups=mesh['req'=16,'tp'=32] {'tp'}, dimensions={0}, use_global_device_ids=true | all-gather | bytes 675840 | tf_op jit(solution)/shard_map/all_gather | solution.py:123
  48.1 0.2 reshape.367
  48.3 0.2 multiply_reduce_fusion
  48.5 0.5 copy-done.3
  49.0 0.2 multiply_convert_fusion
  49.2 0.2 copy-done.1
  49.5 0.3 fusion.6
  49.8 0.1 reshape_reshape.10
  49.9 1.3 %convolution_bitcast_fusion.1 = f32[8,4,64]{2,0,1:T(8,128)S(1)} fusion(bf16[4,8,5120]{2,1,0:T(8,128)(2,1)} %param.16, bf16[64,5120]{1,0:T(8,128)(2,1)S(1)} %multiply_convert_fusion), kind=kOutput, calls=%fused_computation.18 | convolution fusion | flops 20971520 | bytes 991232 | tf_op jit(solution)/shard_map/tm,ehm->het/dot_general | solution.py:132
  51.2 0.1 reshape_reshape.9
  51.3 0.1 select_reduce_fusion.3
  51.4 0.1 select_reduce_fusion.1
  51.5 0.2 reshape.373
  51.9 0.4 reshape.353
  52.3 0.3 copy.58
  52.6 0.3 fusion
  53.1 0.1 copy.60
  53.2 0.6 copy.61
  53.8 0.2 copy.62
  54.2 0.9 copy.70
  55.1 5.1 %all-to-all-start.1 = ((f32[32,32,128]{2,1,0:T(8,128)}), f32[32,32,128]{2,1,0:T(8,128)S(1)}, u32[]{:S(2)}, u32[]{:S(2)}) async-start(f32[32,32,128]{2,1,0:T(8,128)} %bitcast.41), calls=%async_computation.1 | async-start | bytes 1048576 | tf_op jit(solution)/shard_map/all_to_all | solution.py:153
  60.2 1.7 %convolution_add_fusion.1 = f32[64,128]{1,0:T(8,128)S(1)} fusion(bf16[64,5120]{1,0:T(8,128)(2,1)S(1)} %multiply_convert_fusion, bf16[5120,128]{1,0:T(8,128)(2,1)} %param.15, f32[128]{0:T(128)S(1)} %copy-done.5), kind=kOutput, calls=%fused_computation.10 | convolution fusion | flops 83894272 | bytes 1999360 | tf_op jit(solution)/shard_map/dot_general | solution.py:169
  62.0 9.8 %all-to-all-done.1 = f32[32,32,128]{2,1,0:T(8,128)S(1)} async-done(((f32[32,32,128]{2,1,0:T(8,128)}), f32[32,32,128]{2,1,0:T(8,128)S(1)}, u32[]{:S(2)}, u32[]{:S(2)}) %all-to-all-start.1) | async-done | bytes 524320 | tf_op jit(solution)/shard_map/all_to_all | solution.py:153
  71.8 0.3 copy.77
  72.1 0.3 copy.80
  73.0 0.2 copy.63
  73.2 0.2 copy.64
  73.6 0.2 fusion.2
  73.7 0.2 fusion.41
  73.9 0.2 fusion.23
  74.2 0.2 fusion.50
  74.4 0.2 fusion.3
  74.6 0.5 convolution_convert_fusion
  75.2 0.2 reshape.362
  75.4 16.4 %all_to_all.19 = bf16[32,2,5120]{2,1,0:T(2,128)(2,1)S(1)} all-to-all(bf16[32,2,5120]{2,1,0:T(2,128)(2,1)S(1)} %reshape.362), channel_id=1, replica_groups=mesh['req'=16,'tp'=32] {'tp'}, dimensions={0} | all-to-all | bytes 1310720 | tf_op jit(solution)/shard_map/all_to_all | solution.py:196
  91.8 0.5 convert_reduce_fusion
  92.3 0.6 add_convert_fusion
  (52 shorter events, 1.3 us)
Async XLA Ops:
  0.0 74.6 %copy-start = (bf16[128,5120]{1,0:T(8,128)(2,1)S(1)}, bf16[128,5120]{1,0:T(8,128)(2,1)}, u32[]{:S(2)}) copy-start(bf16[128,5120]{1,0:T(8,128)(2,1)} %param.18) | copy-start | bytes 3932164
  0.0 22.1 %copy-start.2 = (bf16[2,5120]{1,0:T(2,128)(2,1)S(1)}, bf16[2,5120]{1,0:T(2,128)(2,1)}, u32[]{:S(2)}) copy-start(bf16[2,5120]{1,0:T(2,128)(2,1)} %param.13) | copy-start | bytes 61444
  6.3 45.2 %all-to-all-start = ((bf16[16,2,3840]{2,1,0:T(2,128)(2,1)}), bf16[16,2,3840]{2,1,0:T(2,128)(2,1)S(1)}, u32[]{:S(2)}, u32[]{:S(2)}) async-start(bf16[16,2,3840]{2,1,0:T(2,128)(2,1)} %reshape.372), calls=%async_computation | async-start | bytes 491520 | tf_op jit(solution)/shard_map/all_to_all | solution.py:110
  48.3 0.7 copy-start.3
  48.5 1.0 %copy-start.1 = (bf16[4,8,5120]{2,1,0:T(8,128)(2,1)S(1)}, bf16[4,8,5120]{2,1,0:T(8,128)(2,1)}, u32[]{:S(2)}) copy-start(bf16[4,8,5120]{2,1,0:T(8,128)(2,1)} %param.17) | copy-start | bytes 983044
  48.5 1.0 %copy-start.4 = (f32[4,8]{1,0:T(4,128)S(1)}, f32[4,8]{1,0:T(4,128)}, u32[]{:S(2)}) copy-start(f32[4,8]{1,0:T(4,128)} %param.20) | copy-start | bytes 388
  49.2 2.1 %copy-start.7 = (s32[1,8]{1,0:T(1,128)S(1)}, s32[1,8]{1,0:T(1,128)}, u32[]{:S(2)}) copy-start(s32[1,8]{1,0:T(1,128)} %param.24) | copy-start | bytes 100
  49.2 2.2 %copy-start.6 = (s32[1,8]{1,0:T(1,128)S(1)}, s32[1,8]{1,0:T(1,128)}, u32[]{:S(2)}) copy-start(s32[1,8]{1,0:T(1,128)} %param.25) | copy-start | bytes 100
  54.2 6.1 %copy-start.5 = (f32[128]{0:T(128)S(1)}, f32[128]{0:T(128)}, u32[]{:S(2)}) copy-start(f32[128]{0:T(128)} %param.19) | copy-start | bytes 1540
  55.1 16.7 %all-to-all-start.1 = ((f32[32,32,128]{2,1,0:T(8,128)}), f32[32,32,128]{2,1,0:T(8,128)S(1)}, u32[]{:S(2)}, u32[]{:S(2)}) async-start(f32[32,32,128]{2,1,0:T(8,128)} %bitcast.41), calls=%async_computation.1 | async-start | bytes 1048576 | tf_op jit(solution)/shard_map/all_to_all | solution.py:153
where the time goes:
time: 93.5 us; the launch traced here: 92.9 us
  blocking collectives  42.3 us (45%)
  starting transfers between devices  20.8 us (22%)
  local copies, waits for them, and re-layouts  10.3 us (11%)
  waiting for transfers between devices  9.85 us (11%)
  matrix products  4.66 us (5%)
  other arithmetic  4.52 us (5%)
    all_gather x1, blocking collectives, shards(): gathered = lax.all_gather(hidden, 'tp', axis=0, tiled=True)  26 us
    all_to_all x1, blocking collectives, shards(): lax.all_to_all(block_terms.reshape(tp_width, tok_rows, block_terms.shape[...  16.4 us
    all_to_all x1, starting transfers between devices, shards(): lax.all_to_all(jnp.tile(bank_piece, (req_width, 1)), 'req', 0, 0, tiled=T...  15.7 us
    all_to_all x1, waiting for transfers between devices, shards(): lax.all_to_all(kv_send, 'tp', 0, 0, tiled=True).reshape(tp_width, -1)  9.85 us
    unnamed x26, local copies, waits for them, and re-layouts  5.74 us
    all_to_all x1, starting transfers between devices, shards(): lax.all_to_all(kv_send, 'tp', 0, 0, tiled=True).reshape(tp_width, -1)  5.08 us
    another operation x1, other arithmetic, shards(): jnp.tile(bank_piece, (req_width, 1))  2.07 us
  transfers between devices with their start and end apart: 2, of which 1 were waited for; matrix products, arithmetic and copies ran while one was open for 5% of the time, Pallas kernels for 0%

commit v1 on v0

--- a/solution.py
+++ b/solution.py
@@ -120,7 +120,9 @@
     group_entry, segment, offset = prompt_layout(prompt_length_list, group_tokens)
     token_adapter = jnp.sum(jnp.where(group_entry, adapter_choice_list[None, :], 0), axis=1)
     adapter_pick = token_adapter[:, None] == jnp.arange(adapter_total, dtype=jnp.int32)[None, :]
-    gathered = lax.all_gather(hidden, "tp", axis=0, tiled=True)
+    gathered = jnp.concatenate(
+        lax.all_to_all(jnp.stack([hidden] * lax.axis_size("tp")), "tp", 0, 0), axis=0
+    )
     normalized_input = rms_rows(gathered, input_norm_gain)
     own_features = lax.dynamic_slice_in_dim(normalized_input, tp_place * feat_slice, feat_slice, 1)
     terms = jnp.dot(

time: 93.5 us -> 97.5 us (1.043)
  blocking collectives: 42.3 us -> 16.3 us
  waiting for transfers between devices: 9.85 us -> 28.3 us
  starting transfers between devices: 20.8 us -> 31.2 us
  other arithmetic: 4.52 us -> 5.66 us
    all_gather x1 -> x0, blocking collectives: 26 us -> none  [shards(): gathered = lax.all_gather(hidden, 'tp', axis=0, tiled=True)]
    all_to_all x0 -> x1, starting transfers between devices: none -> 10.4 us  [shards(): lax.all_to_all(jnp.stack([hidden] * lax.axis_size('tp')), 'tp', 0, 0)]
    all_to_all x1, waiting for transfers between devices: 0.01 us -> 10.3 us  [shards(): lax.all_to_all(jnp.tile(bank_piece, (req_width, 1)), 'req', 0, 0, tiled=T...]
    all_to_all x0 -> x1, waiting for transfers between devices: none -> 8.04 us  [shards(): lax.all_to_all(jnp.stack([hidden] * lax.axis_size('tp')), 'tp', 0, 0)]
    all_to_all x1, starting transfers between devices: 15.7 us -> 13 us  [shards(): lax.all_to_all(jnp.tile(bank_piece, (req_width, 1)), 'req', 0, 0, tiled=T...]
    all_to_all x1, starting transfers between devices: 5.08 us -> 7.81 us  [shards(): lax.all_to_all(kv_send, 'tp', 0, 0, tiled=True).reshape(tp_width, -1)]
    unnamed x26 -> x36, local copies, waits for them, and re-layouts: 5.74 us -> 3.57 us
    another operation x0 -> x1, local copies, waits for them, and re-layouts: none -> 2 us  [shards(): jnp.stack([hidden] * lax.axis_size('tp'))]
  transfers between devices with their start and end apart: 2 -> 3, of which waited for: 1 -> 3; matrix products, arithmetic and copies ran while one was open for 5% -> 10% of each run, Pallas kernels for 0% -> 0%
where the time goes in v1:
time: 97.5 us; the launch traced here: 97 us
  starting transfers between devices  31.2 us (32%)
  waiting for transfers between devices  28.3 us (29%)
  blocking collectives  16.3 us (17%)
  local copies, waits for them, and re-layouts  10.3 us (11%)
  other arithmetic  5.66 us (6%)
  matrix products  4.66 us (5%)
    all_to_all x1, blocking collectives, shards(): lax.all_to_all(block_terms.reshape(tp_width, tok_rows, block_terms.shape[...  16.3 us
    all_to_all x1, starting transfers between devices, shards(): lax.all_to_all(jnp.tile(bank_piece, (req_width, 1)), 'req', 0, 0, tiled=T...  13 us
    all_to_all x1, starting transfers between devices, shards(): lax.all_to_all(jnp.stack([hidden] * lax.axis_size('tp')), 'tp', 0, 0)  10.4 us
    all_to_all x1, waiting for transfers between devices, shards(): lax.all_to_all(jnp.tile(bank_piece, (req_width, 1)), 'req', 0, 0, tiled=T...  10.3 us
    all_to_all x1, waiting for transfers between devices, shards(): lax.all_to_all(kv_send, 'tp', 0, 0, tiled=True).reshape(tp_width, -1)  9.95 us
    all_to_all x1, waiting for transfers between devices, shards(): lax.all_to_all(jnp.stack([hidden] * lax.axis_size('tp')), 'tp', 0, 0)  8.04 us
    all_to_all x1, starting transfers between devices, shards(): lax.all_to_all(kv_send, 'tp', 0, 0, tiled=True).reshape(tp_width, -1)  7.81 us
    unnamed x36, local copies, waits for them, and re-layouts  3.57 us
  transfers between devices with their start and end apart: 3, of which 3 were waited for; matrix products, arithmetic and copies ran while one was open for 10% of the time, Pallas kernels for 0%

profile of v1, /device:TPU:1, one launch (start us, length us, event | category | flops | bytes accessed | tf_op | source)
XLA Modules:
  0.0 97.0 jit_solution(16961229776020003152)
XLA Ops:
  0.0 2.0 %stack.2 = bf16[32,2,5120]{2,1,0:T(2,128)(2,1)} broadcast(bf16[2,5120]{1,0:T(2,128)(2,1)} %param.13), dimensions={1,2} | broadcast | bytes 675840 | tf_op jit(solution)/shard_map/stack | solution.py:124
  2.0 10.4 %all-to-all-start = ((bf16[32,2,5120]{2,1,0:T(2,128)(2,1)}), bf16[32,2,5120]{2,1,0:T(2,128)(2,1)S(1)}, u32[]{:S(2)}, u32[]{:S(2)}) async-start(bf16[32,2,5120]{2,1,0:T(2,128)(2,1)} %stack.2), calls=%async_computation | async-start | bytes 1310720 | tf_op jit(solution)/shard_map/all_to_all | solution.py:124
  12.5 0.1 copy.56
  12.6 0.1 reshape.364
  12.8 0.1 reshape.366
  13.0 0.3 tile.2
  13.3 0.5 broadcast.226
  13.8 2.1 %reduce.6 = bf16[16,7680]{1,0:T(8,128)(2,1)S(1)} reduce(bf16[16,1,7680]{2,1,0:T(2,128)(2,1)S(1)} %tile.2, bf16[]{:T(256)} %broadcast.226), dimensions={1}, to_apply=%tile.2.reduce_sub_computation | reduce | bytes 491522 | tf_op jit(solution)/shard_map/tile | solution.py:110
  15.9 0.8 reshape.384
  16.7 0.1 select_reduce_fusion.3
  16.8 0.7 select_reduce_fusion.1
  17.5 8.0 %all-to-all-done = bf16[32,2,5120]{2,1,0:T(2,128)(2,1)S(1)} async-done(((bf16[32,2,5120]{2,1,0:T(2,128)(2,1)}), bf16[32,2,5120]{2,1,0:T(2,128)(2,1)S(1)}, u32[]{:S(2)}, u32[]{:S(2)}) %all-to-all-start) | async-done | bytes 655392 | tf_op jit(solution)/shard_map/all_to_all | solution.py:124
  25.5 13.0 %all-to-all-start.1 = ((bf16[16,2,3840]{2,1,0:T(2,128)(2,1)}), bf16[16,2,3840]{2,1,0:T(2,128)(2,1)S(1)}, u32[]{:S(2)}, u32[]{:S(2)}) async-start(bf16[16,2,3840]{2,1,0:T(2,128)(2,1)} %reshape.384), calls=%async_computation.1 | async-start | bytes 491520 | tf_op jit(solution)/shard_map/all_to_all | solution.py:110
  38.5 0.8 multiply_reduce_fusion
  39.3 0.1 rsqrt.12
  39.4 0.2 reshape.377
  39.6 0.2 multiply_convert_fusion
  39.8 0.8 copy-done.1
  40.6 0.3 fusion.6
  40.9 0.1 reshape_reshape.10
  41.0 1.3 %convolution_bitcast_fusion.1 = f32[8,4,64]{2,0,1:T(8,128)S(1)} fusion(bf16[4,8,5120]{2,1,0:T(8,128)(2,1)} %param.16, bf16[64,5120]{1,0:T(8,128)(2,1)S(1)} %multiply_convert_fusion), kind=kOutput, calls=%fused_computation.18 | convolution fusion | flops 20971520 | bytes 991232 | tf_op jit(solution)/shard_map/tm,ehm->het/dot_general | solution.py:134
  42.3 0.1 reshape_reshape.9
  42.4 10.3 %all-to-all-done.1 = bf16[16,2,3840]{2,1,0:T(2,128)(2,1)S(1)} async-done(((bf16[16,2,3840]{2,1,0:T(2,128)(2,1)}), bf16[16,2,3840]{2,1,0:T(2,128)(2,1)S(1)}, u32[]{:S(2)}, u32[]{:S(2)}) %all-to-all-start.1) | async-done | bytes 245792 | tf_op jit(solution)/shard_map/all_to_all | solution.py:110
  52.7 0.2 reshape.385
  53.0 0.4 reshape.367
  53.5 0.3 copy.58
  53.8 0.3 fusion
  54.3 0.1 copy.60
  54.4 0.6 copy.61
  55.0 0.2 copy.62
  55.4 0.9 copy.70
  56.3 7.8 %all-to-all-start.2 = ((f32[32,32,128]{2,1,0:T(8,128)}), f32[32,32,128]{2,1,0:T(8,128)S(1)}, u32[]{:S(2)}, u32[]{:S(2)}) async-start(f32[32,32,128]{2,1,0:T(8,128)} %bitcast.40), calls=%async_computation.2 | async-start | bytes 1048576 | tf_op jit(solution)/shard_map/all_to_all | solution.py:155
  64.2 1.7 %convolution_add_fusion.1 = f32[64,128]{1,0:T(8,128)S(1)} fusion(bf16[64,5120]{1,0:T(8,128)(2,1)S(1)} %multiply_convert_fusion, bf16[5120,128]{1,0:T(8,128)(2,1)} %param.15, f32[128]{0:T(128)S(1)} %copy-done.8), kind=kOutput, calls=%fused_computation.10 | convolution fusion | flops 83894272 | bytes 1999360 | tf_op jit(solution)/shard_map/dot_general | solution.py:171
  65.9 9.9 %all-to-all-done.2 = f32[32,32,128]{2,1,0:T(8,128)S(1)} async-done(((f32[32,32,128]{2,1,0:T(8,128)}), f32[32,32,128]{2,1,0:T(8,128)S(1)}, u32[]{:S(2)}, u32[]{:S(2)}) %all-to-all-start.2) | async-done | bytes 524320 | tf_op jit(solution)/shard_map/all_to_all | solution.py:155
  75.8 0.3 copy.77
  76.2 0.3 copy.80
  77.0 0.2 copy.63
  77.2 0.2 copy.64
  77.6 0.2 fusion.2
  77.8 0.2 fusion.41
  78.0 0.2 fusion.23
  78.2 0.2 fusion.50
  78.5 0.2 fusion.3
  78.7 0.5 convolution_convert_fusion
  79.2 0.2 reshape.376
  79.5 16.3 %all_to_all.24 = bf16[32,2,5120]{2,1,0:T(2,128)(2,1)S(1)} all-to-all(bf16[32,2,5120]{2,1,0:T(2,128)(2,1)S(1)} %reshape.376), channel_id=1, replica_groups=mesh['req'=16,'tp'=32] {'tp'}, dimensions={0} | all-to-all | bytes 1310720 | tf_op jit(solution)/shard_map/all_to_all | solution.py:198
  95.8 0.5 convert_reduce_fusion
  96.3 0.6 add_convert_fusion
  (65 shorter events, 1.5 us)
Async XLA Ops:
  0.0 78.7 %copy-start = (bf16[128,5120]{1,0:T(8,128)(2,1)S(1)}, bf16[128,5120]{1,0:T(8,128)(2,1)}, u32[]{:S(2)}) copy-start(bf16[128,5120]{1,0:T(8,128)(2,1)} %param.18) | copy-start | bytes 3932164
  0.0 12.5 %copy-start.4 = (bf16[1,160,32]{1,2,0:T(8,128)(2,1)S(1)}, bf16[1,160,32]{1,2,0:T(8,128)(2,1)}, u32[]{:S(2)}) copy-start(bf16[1,160,32]{1,2,0:T(8,128)(2,1)} %param.21) | copy-start | bytes 30724
  0.0 12.7 %copy-start.5 = (bf16[1,16,4,8]{1,3,2,0:T(8,128)(2,1)S(1)}, bf16[1,16,4,8]{1,3,2,0:T(8,128)(2,1)}, u32[]{:S(2)}) copy-start(bf16[1,16,4,8]{1,3,2,0:T(8,128)(2,1)} %param.23) | copy-start | bytes 3076
  0.0 12.9 %copy-start.6 = (bf16[1,16,128]{2,1,0:T(8,128)(2,1)S(1)}, bf16[1,16,128]{2,1,0:T(8,128)(2,1)}, u32[]{:S(2)}) copy-start(bf16[1,16,128]{2,1,0:T(8,128)(2,1)} %param.22) | copy-start | bytes 12292
  2.0 23.5 %all-to-all-start = ((bf16[32,2,5120]{2,1,0:T(2,128)(2,1)}), bf16[32,2,5120]{2,1,0:T(2,128)(2,1)S(1)}, u32[]{:S(2)}, u32[]{:S(2)}) async-start(bf16[32,2,5120]{2,1,0:T(2,128)(2,1)} %stack.2), calls=%async_computation | async-start | bytes 1310720 | tf_op jit(solution)/shard_map/all_to_all | solution.py:124
  12.5 4.2 %copy-start.12 = (s32[1,8]{1,0:T(1,128)S(1)}, s32[1,8]{1,0:T(1,128)}, u32[]{:S(2)}) copy-start(s32[1,8]{1,0:T(1,128)} %param.24) | copy-start | bytes 100
  12.5 4.3 %copy-start.9 = (s32[1,8]{1,0:T(1,128)S(1)}, s32[1,8]{1,0:T(1,128)}, u32[]{:S(2)}) copy-start(s32[1,8]{1,0:T(1,128)} %param.25) | copy-start | bytes 100
  25.5 27.2 %all-to-all-start.1 = ((bf16[16,2,3840]{2,1,0:T(2,128)(2,1)}), bf16[16,2,3840]{2,1,0:T(2,128)(2,1)S(1)}, u32[]{:S(2)}, u32[]{:S(2)}) async-start(bf16[16,2,3840]{2,1,0:T(2,128)(2,1)} %reshape.384), calls=%async_computation.1 | async-start | bytes 491520 | tf_op jit(solution)/shard_map/all_to_all | solution.py:110
  38.5 1.1 %copy-start.3 = (f32[5120]{0:T(1024)S(1)}, f32[5120]{0:T(1024)}, u32[]{:S(2)}) copy-start(f32[5120]{0:T(1024)} %param.14) | copy-start | bytes 61444
  39.6 1.0 %copy-start.1 = (bf16[4,8,5120]{2,1,0:T(8,128)(2,1)S(1)}, bf16[4,8,5120]{2,1,0:T(8,128)(2,1)}, u32[]{:S(2)}) copy-start(bf16[4,8,5120]{2,1,0:T(8,128)(2,1)} %param.17) | copy-start | bytes 983044
  39.6 1.0 copy-start.7
  55.3 8.8 %copy-start.11 = (s32[64]{0:T(128)S(1)}, s32[64]{0:T(128)}, u32[]{:S(2)}) copy-start(s32[64]{0:T(128)} %get-tuple-element.6) | copy-start | bytes 772
  55.4 8.8 %copy-start.8 = (f32[128]{0:T(128)S(1)}, f32[128]{0:T(128)}, u32[]{:S(2)}) copy-start(f32[128]{0:T(128)} %param.19) | copy-start | bytes 1540
  56.3 19.5 %all-to-all-start.2 = ((f32[32,32,128]{2,1,0:T(8,128)}), f32[32,32,128]{2,1,0:T(8,128)S(1)}, u32[]{:S(2)}, u32[]{:S(2)}) async-start(f32[32,32,128]{2,1,0:T(8,128)} %bitcast.40), calls=%async_computation.2 | async-start | bytes 1048576 | tf_op jit(solution)/shard_map/all_to_all | solution.py:155
  76.5 1.7 %copy-start.10 = (s32[64]{0:T(128)S(1)}, s32[64]{0:T(128)}, u32[]{:S(2)}) copy-start(s32[64]{0:T(128)} %get-tuple-element.5) | copy-start | bytes 772
  79.5 16.9 %copy-start.2 = (bf16[2,5120]{1,0:T(2,128)(2,1)S(1)}, bf16[2,5120]{1,0:T(2,128)(2,1)}, u32[]{:S(2)}) copy-start(bf16[2,5120]{1,0:T(2,128)(2,1)} %param.13) | copy-start | bytes 61444
